TPU v7x, 32 devices: a whole 2x2x4 slice. The times are simulated.
32 devices in a mesh: space: 8 (over y, x, core), species: 4 (over z).
Axes of the slice: x: 2, y: 2, z: 4, core: 2. Of those that a mesh axis runs over, the one named last changes fastest.
Arguments:
- cotangent: bfloat16 [4, 400, 20, 1024], P('species', None, None, 'space'), may hold values from -6 to 6
- freq: float32 [4], P('species'), may hold values from 0.2 to 0.9
- ratio: float32 [4], P('species'), may hold values from 0.5 to 1
- coupling: float32 [4, 4, 13], replicated, may hold values from 0.1 to 0.6
- wall: int32 [1024], P('space'), may hold values 0 or 1
- inlet: int32 [1024], P('space'), may hold values 0 or 1
- face_type: int32 [2, 8], P(None, 'space'), may hold values from 0 to 1
Outputs:
- grad_state: bfloat16 [4, 400, 20, 1024], P('species', None, None, 'space')
Inputs may be any that keep to these rules, and one draw needn't show every extreme that they name: `wall`: 1 marks a solid cell. `inlet`: 1 marks an inlet cell. `face_type`: 0 is a specular wall, 1 a reversing wall.
All inputs are finite; a program needn't handle non-finite values. No bound on the sum of `wall` or of `inlet` on one device may be relied on, other than what follows from the above.
Results may differ from a plain program's by a relative error of at most 0.0049.
Values may be sent and summed in bfloat16 or wider, within the bound.
No kernel may reach another device: no remote copies, remote signals or barrier semaphores. Data moves between devices by JAX's collectives and lax.ppermute only.
A program may use at most 64 MiB of HBM per device.

v0:
```python
import math

import numpy as np
import jax
import jax.numpy as jnp
from jax import lax
from jax.experimental import pallas as pl
from jax.experimental.pallas import tpu as pltpu
from jax.sharding import PartitionSpec as P


NZ = 128

courant_max = 0.45
node_reach = 2.85


def passed_along(value, axis, steps):
    count = lax.axis_size(axis)
    pairs = [(source, (source + steps) % count) for source in range(count)]
    return lax.ppermute(value, axis, pairs)


def velocity_tables(node_count):
    pair_count = node_count * node_count
    spacing = 2.0 * node_reach / (node_count - 1)
    node_line = (np.arange(node_count, dtype=np.float64) - 0.5 * (node_count - 1)) * spacing
    grid_shape = (pair_count, node_count)
    along_x = np.broadcast_to(np.repeat(node_line, node_count)[:, None], grid_shape)
    along_y = np.broadcast_to(np.tile(node_line, node_count)[:, None], grid_shape)
    along_z = np.broadcast_to(node_line[None, :], grid_shape)
    square = along_x * along_x + along_y * along_y + along_z * along_z
    heat_term = square - 2.5
    functions = [
        np.ones(grid_shape),
        along_x,
        along_y,
        along_z,
        square - 1.5,
        along_x * along_y,
        along_x * along_z,
        along_y * along_z,
        along_x * along_x - along_y * along_y,
        along_y * along_y - along_z * along_z,
        along_x * heat_term,
        along_y * heat_term,
        along_z * heat_term,
    ]
    stacked = np.stack(functions)
    basis = stacked / np.sqrt(np.mean(stacked * stacked, axis=(1, 2), keepdims=True))
    weights = np.exp(-square) * (spacing * spacing * spacing) / math.pi**1.5
    recon = basis * weights[None]
    return node_line, basis, recon


def bf16_split(table, parts):
    rest = np.asarray(table, np.float64)
    pieces = []
    for _ in range(parts):
        piece = rest.astype(np.float32).astype(jnp.bfloat16).astype(np.float64)
        pieces.append(piece)
        rest = rest - piece
    return pieces


def on_device(cotangent, freq, ratio, coupling, wall, inlet, face_type):
    pair_count = cotangent.shape[1]
    node_count = cotangent.shape[2]
    cell_count = cotangent.shape[3]
    assert cell_count == NZ
    half = pair_count // 2
    moment_count = coupling.shape[2]
    species_count = lax.axis_size("species")

    node_line, basis, recon = velocity_tables(node_count)
    basis_k = np.transpose(basis, (0, 2, 1)).reshape(moment_count, node_count * pair_count)
    basis_parts = np.concatenate(bf16_split(basis_k, 3), axis=0)
    basis_parts = jnp.asarray(basis_parts.astype(jnp.bfloat16))
    weight_k = (recon[0] / basis[0]).T.reshape(-1).astype(np.float32)

    field_in = jnp.transpose(cotangent[0], (1, 0, 2))
    upper_in = field_in[:, half:, :]
    lower_in = field_in[:, :half, :]
    got_next = passed_along(upper_in, "space", -1)
    got_prev = passed_along(lower_in, "space", 1)

    open_cells = (1 - wall).astype(jnp.float32)
    keep_upper = open_cells * (1.0 - inlet.astype(jnp.float32))
    upward = (jnp.arange(pair_count) >= half)[None, :, None]
    keep = jnp.where(upward, keep_upper[None, None, :], open_cells[None, None, :])
    masked = field_in * keep.astype(jnp.bfloat16)
    parts = jnp.dot(
        basis_parts,
        masked.reshape(node_count * pair_count, cell_count),
        preferred_element_type=jnp.float32,
    )
    moments = parts[:moment_count] + parts[moment_count : 2 * moment_count] + parts[2 * moment_count :]

    species_index = lax.axis_index("species")
    row_k = lax.dynamic_index_in_dim(coupling, species_index, axis=0, keepdims=False)
    own_weight = lax.dynamic_index_in_dim(row_k, species_index, axis=0, keepdims=False)
    cross = own_weight[:, None] * moments
    for shift in range(1, species_count):
        source = (species_index - shift) % species_count
        other = passed_along(moments, "species", shift)
        weight = lax.dynamic_index_in_dim(row_k, source, axis=0, keepdims=False)
        cross = cross + weight[:, None] * other

    rows = 16
    assert moment_count + 2 < rows
    packet = jnp.concatenate(
        [
            cross,
            open_cells[None],
            keep_upper[None],
            jnp.zeros((rows - moment_count - 2, cell_count), jnp.float32),
        ],
        axis=0,
    )
    packet_next = passed_along(packet, "space", -1)
    packet_prev = passed_along(packet, "space", 1)

    rate_value = freq[0]
    scale_factor = courant_max * ratio[0] / node_reach
    line = jnp.asarray(node_line.astype(np.float32))
    pair_line = jnp.repeat(line, node_count)
    adv_x = jnp.abs(scale_factor * pair_line)
    adv_z = jnp.abs(scale_factor * line)
    columns = jnp.broadcast_to(
        jnp.stack([1.0 - adv_x, adv_x])[:, :, None], (2, pair_count, cell_count)
    )
    scalars = jnp.concatenate(
        [adv_z, jnp.zeros((31 - node_count,), jnp.float32), (1.0 - rate_value)[None]]
    )
    faces = face_type[:, 0]

    lanes = 128
    recon_halves = jnp.asarray(packed_recon(recon, rows, lanes))

    flip_rows = lax.broadcasted_iota(jnp.int32, (pair_count, pair_count), 0)
    flip_cols = lax.broadcasted_iota(jnp.int32, (pair_count, pair_count), 1)
    flip = (flip_rows + flip_cols == pair_count - 1).astype(jnp.bfloat16)

    partial = own_kernel(field_in, recon_halves, packet, columns, flip, scalars, faces)
    out = halo_kernel(
        partial, got_next, got_prev, recon_halves, packet_next, packet_prev,
        columns, scalars,
    )
    return jnp.transpose(out, (1, 0, 2))[None]


def packed_recon(recon, rows, lanes):
    moment_count, pair_count, node_count = recon.shape
    half = pair_count // 2
    table = np.transpose(recon, (2, 1, 0))
    parts = bf16_split(table, 3)
    order = [0, 0, 1, 0, 1, 2]
    packed = np.zeros((node_count, pair_count, lanes), np.float32)
    for block, part in enumerate(order):
        packed[:, :, block * rows : block * rows + moment_count] = parts[part]
    packed = packed.reshape(node_count, 2, half, lanes)
    return packed.astype(jnp.bfloat16)


def cross_matrix(packet, moment_count):
    rows = packet.shape[0]
    row = lax.broadcasted_iota(jnp.int32, packet.shape, 0)
    values = jnp.where(row < moment_count, packet, 0.0)
    c1 = values.astype(jnp.bfloat16)
    left = values - c1.astype(jnp.float32)
    c2 = left.astype(jnp.bfloat16)
    c3 = (left - c2.astype(jnp.float32)).astype(jnp.bfloat16)
    pad = jnp.zeros((128 - 6 * rows, packet.shape[1]), jnp.bfloat16)
    return jnp.concatenate([c1, c2, c1, c3, c2, c1, pad], axis=0)


def own_kernel(field_in, recon_halves, packet, columns, flip, scalars, faces):
    node_count, pair_count, cell_count = field_in.shape
    half = pair_count // 2
    steps = node_count // 2
    moment_count = packet.shape[0] - 3
    group = 5 if steps % 5 == 0 else 1
    blocks = steps // group

    def kernel(sc_ref, face_ref, cot_lo, cot_hi, rec_lo, rec_hi, pk_ref, col_ref, flip_ref, out_ref):
        b = pl.program_id(0)
        row = lax.broadcasted_iota(jnp.int32, (pair_count, cell_count), 0)
        lane = lax.broadcasted_iota(jnp.int32, (pair_count, cell_count), 1)
        pk = pk_ref[...]
        rate = sc_ref[31]
        keep = rate * jnp.where(row >= half, pk[moment_count + 1 : moment_count + 2, :], pk[moment_count : moment_count + 1, :])
        own = cross_matrix(pk, moment_count)
        base = col_ref[0]
        face_a = face_ref[0] == 1
        face_b = face_ref[1] == 1

        def relax(values, rec_ref, at):
            rebuilt = jnp.concatenate(
                [
                    jnp.dot(rec_ref[at, 0], own, preferred_element_type=jnp.float32),
                    jnp.dot(rec_ref[at, 1], own, preferred_element_type=jnp.float32),
                ],
                axis=0,
            )
            return (keep * values.astype(jnp.float32) + rebuilt).astype(jnp.bfloat16)

        def one(t, carry):
            u = group - 1 - t
            j = b * group + t
            relaxed_a = relax(cot_lo[t], rec_lo, t)
            relaxed_b = relax(cot_hi[u], rec_hi, u)
            edges = jnp.where(lane == 0, relaxed_b, relaxed_a)
            flipped = jnp.dot(flip_ref[...], edges, preferred_element_type=jnp.float32)
            edges32 = edges.astype(jnp.float32)
            source_a = jnp.where(face_a, flipped, edges32)
            source_b = jnp.where(face_b, flipped, edges32)
            ra = relaxed_a.astype(jnp.float32)
            rb = relaxed_b.astype(jnp.float32)
            near_a = jnp.where(lane == 0, source_a, pltpu.roll(ra, 1, 1))
            near_b = jnp.where(lane == cell_count - 1, source_b, pltpu.roll(rb, cell_count - 1, 1))
            zw_a = sc_ref[j]
            zw_b = sc_ref[node_count - 1 - j]
            out_ref[0, t] = (base - zw_a) * ra + zw_a * near_a
            out_ref[1, t] = (base - zw_b) * rb + zw_b * near_b
            return carry

        lax.fori_loop(0, group, one, 0)

    block = (group, pair_count, cell_count)
    smem = pl.BlockSpec(memory_space=pltpu.SMEM)
    in_specs = [
        smem,
        smem,
        pl.BlockSpec(block, lambda b: (b, 0, 0)),
        pl.BlockSpec(block, lambda b: (2 * blocks - 1 - b, 0, 0)),
        pl.BlockSpec((group, 2, half, recon_halves.shape[3]), lambda b: (b, 0, 0, 0)),
        pl.BlockSpec((group, 2, half, recon_halves.shape[3]), lambda b: (2 * blocks - 1 - b, 0, 0, 0)),
        pl.BlockSpec(packet.shape, lambda b: (0, 0)),
        pl.BlockSpec((1, pair_count, cell_count), lambda b: (0, 0, 0)),
        pl.BlockSpec(flip.shape, lambda b: (0, 0)),
    ]
    return pl.pallas_call(
        kernel,
        grid=(blocks,),
        in_specs=in_specs,
        out_specs=pl.BlockSpec((2,) + block, lambda b: (0, b, 0, 0)),
        out_shape=jax.ShapeDtypeStruct((2, steps, pair_count, cell_count), jnp.float32),
        compiler_params=pltpu.CompilerParams(
            dimension_semantics=("arbitrary",), vmem_limit_bytes=60 * 1024 * 1024
        ),
    )(scalars, faces, field_in, field_in, recon_halves, recon_halves, packet, columns, flip)


def halo_kernel(partial, got_next, got_prev, recon_halves, packet_next, packet_prev, columns, scalars):
    node_count, half, cell_count = got_next.shape
    pair_count = 2 * half
    steps = node_count // 2
    moment_count = packet_next.shape[0] - 3
    group = 5 if steps % 5 == 0 else 1
    blocks = node_count // group
    lower_blocks = steps // group

    def kernel(sc_ref, part_ref, nxt_ref, prv_ref, rec_ref, pn_ref, pp_ref, col_ref, out_ref):
        i = pl.program_id(0)
        rate = sc_ref[31]
        pn = pn_ref[...]
        pp = pp_ref[...]
        next_mat = cross_matrix(pn, moment_count)
        prev_mat = cross_matrix(pp, moment_count)
        keep_up = rate * pn[moment_count + 1 : moment_count + 2, :]
        keep_down = rate * pp[moment_count : moment_count + 1, :]
        side = col_ref[0]

        def run(mirrored):
            def one(t, carry):
                up = jnp.dot(rec_ref[t, 1], next_mat, preferred_element_type=jnp.float32)
                down = jnp.dot(rec_ref[t, 0], prev_mat, preferred_element_type=jnp.float32)
                up = (keep_up * nxt_ref[t].astype(jnp.float32) + up).astype(jnp.bfloat16)
                down = (keep_down * prv_ref[t].astype(jnp.float32) + down).astype(jnp.bfloat16)
                shifted = jnp.concatenate([down.astype(jnp.float32), up.astype(jnp.float32)], axis=0)
                part = part_ref[0, group - 1 - t] if mirrored else part_ref[0, t]
                out_ref[t] = (part + side * shifted).astype(jnp.bfloat16)
                return carry

            lax.fori_loop(0, group, one, 0)

        @pl.when(i < lower_blocks)
        def _():
            run(False)

        @pl.when(i >= lower_blocks)
        def _():
            run(True)

    block = (group, pair_count, cell_count)
    smem = pl.BlockSpec(memory_space=pltpu.SMEM)
    in_specs = [
        smem,
        pl.BlockSpec(
            (1,) + block,
            lambda i: (
                jnp.where(i < lower_blocks, 0, 1),
                jnp.where(i < lower_blocks, i, blocks - 1 - i),
                0,
                0,
            ),
        ),
        pl.BlockSpec((group, half, cell_count), lambda i: (i, 0, 0)),
        pl.BlockSpec((group, half, cell_count), lambda i: (i, 0, 0)),
        pl.BlockSpec((group, 2, half, recon_halves.shape[3]), lambda i: (i, 0, 0, 0)),
        pl.BlockSpec(packet_next.shape, lambda i: (0, 0)),
        pl.BlockSpec(packet_prev.shape, lambda i: (0, 0)),
        pl.BlockSpec((1, pair_count, cell_count), lambda i: (1, 0, 0)),
    ]
    return pl.pallas_call(
        kernel,
        grid=(blocks,),
        in_specs=in_specs,
        out_specs=pl.BlockSpec(block, lambda i: (i, 0, 0)),
        out_shape=jax.ShapeDtypeStruct((node_count, pair_count, cell_count), jnp.bfloat16),
        compiler_params=pltpu.CompilerParams(
            dimension_semantics=("arbitrary",), vmem_limit_bytes=60 * 1024 * 1024
        ),
    )(scalars, partial, got_next, got_prev, recon_halves, packet_next, packet_prev, columns)


def solution(mesh):
    in_specs = (
        P("species", None, None, "space"),
        P("species"),
        P("species"),
        P(),
        P("space"),
        P("space"),
        P(None, "space"),
    )
    out_specs = P("species", None, None, "space")

    return jax.shard_map(on_device, mesh=mesh, in_specs=in_specs, out_specs=out_specs, check_vma=False)
```

profile of v0, /device:TPU:1, one launch (start us, length us, event | category | flops | bytes accessed | tf_op | source)
XLA Modules:
  0.0 48.0 jit_solution(8077293116731672460)
XLA Ops:
  0.0 0.7 %subtract_convert_fusion = (bf16[128]{0:T(256)(128)(2,1)S(1)}, f32[1,128]{1,0:T(1,128)S(1)}) fusion(s32[128]{0:T(128)} %param.14), kind=kLoop, calls=%fused_computation.21 | loop fusion | flops 384 | bytes 1280 | tf_op jit(solution)/shard_map/convert_element_type | solution.py:87
  0.7 0.7 %subtract_multiply_fusion = f32[128]{0:T(128)S(1)} fusion(s32[128]{0:T(128)} %param.15, s32[128]{0:T(128)} %param.14), kind=kLoop, calls=%fused_computation.20 | loop fusion | flops 640 | bytes 1536 | tf_op jit(solution)/shard_map/mul | solution.py:88
  1.3 0.1 select_convert_fusion
  1.5 0.0 copy-start.3
  1.5 1.8 %broadcast_multiply_fusion = bf16[20,400,128]{2,1,0:T(8,128)(2,1)S(1)} fusion(bf16[400,128]{1,0:T(8,128)(2,1)S(1)} %select_convert_fusion, bf16[1,400,20,128]{3,1,2,0:T(8,128)(2,1)} %param.10), kind=kLoop, calls=%fused_computation | loop fusion | flops 1024000 | bytes 4198400 | tf_op jit(solution)/shard_map/mul | solution.py:91
  3.3 0.0 copy-start
  3.3 0.0 copy-done.3
  3.3 0.5 %fusion.7 = f32[39,128]{1,0:T(8,128)S(1)} fusion(bf16[39,8000]{1,0:T(8,128)(2,1)S(1)} %copy-done.3, bf16[8000,128]{1,0:T(8,128)(2,1)S(1)} %bitcast.27), kind=kOutput, calls=%fused_computation.25 | convolution fusion | flops 79872000 | bytes 2691968 | tf_op jit(solution)/shard_map/dot_general | solution.py:92
  3.8 3.2 %collective-permute-start.1 = (f32[13,128]{1,0:T(8,128)S(1)}, f32[13,128]{1,0:T(8,128)S(1)}, u32[]{:S(2)}, u32[]{:S(2)}) collective-permute-start(f32[13,128]{1,0:T(8,128)S(1)} %slice_add_fusion), channel_id=1, source_target_pairs={{0,2},{1,3},{2,0},{3,1},{4,6},{5,7},{6,4},{7,5},{8,10},{9,11},{10,... | collective-permute-start | bytes 19976 | tf_op jit(solution)/shard_map/ppermute | solution.py:21
  7.0 1.3 %collective-permute-start = (f32[13,128]{1,0:T(8,128)S(1)}, f32[13,128]{1,0:T(8,128)S(1)}, u32[]{:S(2)}, u32[]{:S(2)}) collective-permute-start(f32[13,128]{1,0:T(8,128)S(1)} %slice_add_fusion), channel_id=1, source_target_pairs={{0,1},{1,2},{2,3},{3,0},{4,5},{5,6},{6,7},{7,4},{8,9},{9,10},{10,1... | collective-permute-start | bytes 19976 | tf_op jit(solution)/shard_map/ppermute | solution.py:21
  8.3 2.0 %collective-permute-start.2 = (f32[13,128]{1,0:T(8,128)S(1)}, f32[13,128]{1,0:T(8,128)S(1)}, u32[]{:S(2)}, u32[]{:S(2)}) collective-permute-start(f32[13,128]{1,0:T(8,128)S(1)} %slice_add_fusion), channel_id=1, source_target_pairs={{0,3},{1,0},{2,1},{3,2},{4,7},{5,4},{6,5},{7,6},{8,11},{9,8},{10,9... | collective-permute-start | bytes 19976 | tf_op jit(solution)/shard_map/ppermute | solution.py:21
  10.3 0.0 copy-done
  10.3 0.0 copy-start.7
  10.3 1.1 %fusion.6 = (bf16[20,200,128]{2,1,0:T(8,128)(2,1)}, bf16[20,200,128]{2,1,0:T(8,128)(2,1)S(1)}) fusion(bf16[20,400,128]{2,1,0:T(8,128)(2,1)S(1)} %bitcast.26), kind=kLoop, calls=%fused_computation.24 | loop fusion | bytes 4096000 | tf_op jit(solution)/shard_map/slice | solution.py:83
  11.4 2.6 %collective-permute-start.4 = (bf16[20,200,128]{2,1,0:T(8,128)(2,1)}, bf16[20,200,128]{2,1,0:T(8,128)(2,1)S(1)}, u32[]{:S(2)}, u32[]{:S(2)}) collective-permute-start(bf16[20,200,128]{2,1,0:T(8,128)(2,1)} %get-tuple-element.5), channel_id=1, source_target_pairs={{0,4},{4,8},{8,12},{12,16},{16,20},{20,24},{24,28},{28,0},{1,5},{5... | collective-permute-start | bytes 3072008 | tf_op jit(solution)/shard_map/ppermute | solution.py:21
  14.0 0.0 collective-permute-start.3
  14.7 0.0 copy-done.7
  14.7 0.1 broadcast_in_dim.59
  14.8 0.1 abs.20
  14.9 0.8 %fusion.flip_ref = bf16[400,400]{1,0:T(8,128)(2,1)} fusion(), kind=kLoop, calls=%fused_computation.2 | loop fusion | flops 480000 | bytes 320000 | tf_op jit(solution)/shard_map/convert_element_type | solution.py:142
  15.7 0.8 %fusion.1 = (f32[13]{0:T(128)S(1)}, f32[13]{0:T(128)S(1)}, f32[13]{0:T(128)S(1)}, f32[13]{0:T(128)S(1)}) fusion(f32[4,4,13]{2,1,0:T(4,128)} %param.13, s32[]{:T(128)S(6)} %select_n.48, s32[]{:T(128)S(6)} %select_n.52, s32[]{:T(128)S(6)} %select_n.58, s32[]{:T(128)S(6)} %select_n.55), kind=kLoop, calls=%fused_computation.15 | loop fusion | bytes 432 | tf_op jit(solution)/shard_map/mul | solution.py:102
  17.2 0.1 pad.5.clone
  17.3 0.0 collective-permute-done.1
  17.3 0.0 collective-permute-done
  17.3 0.0 collective-permute-done.2
  17.3 0.1 multiply_add_fusion
  17.4 0.1 maximum_maximum_fusion.pk_ref
  17.4 0.0 copy-start.4
  17.4 1.7 %collective-permute-start.6 = (f32[16,128]{1,0:T(8,128)S(1)}, f32[16,128]{1,0:T(8,128)S(1)}, u32[]{:S(2)}, u32[]{:S(2)}) collective-permute-start(f32[16,128]{1,0:T(8,128)S(1)} %maximum_maximum_fusion.pk_ref), channel_id=1, source_target_pairs={{0,4},{4,8},{8,12},{12,16},{16,20},{20,24},{24,28},{28,0},{1,5},{5... | collective-permute-start | bytes 24584 | tf_op jit(solution)/shard_map/ppermute | solution.py:21
  19.2 0.0 collective-permute-start.5
  19.2 0.6 %pad_maximum_fusion.1.sc_ref = f32[32]{0:T(128)} fusion(f32[1]{0:T(128)S(6)} %sub.38, f32[11]{0:T(128)S(1)} %broadcast.71, f32[20]{0:T(128)S(1)} %multiply_abs_fusion), kind=kLoop, calls=%fused_computation.19 | loop fusion | flops 64 | bytes 256 | tf_op jit(solution)/shard_map/concatenate | solution.py:132
  19.8 0.9 %broadcast_in_dim.60.col_ref = f32[2,400,128]{2,1,0:T(8,128)} broadcast(f32[2,400]{1,0:T(2,128)S(1)} %pad_maximum_fusion), dimensions={0,1} | broadcast | bytes 412800 | tf_op jit(solution)/shard_map/broadcast_in_dim | solution.py:129
  20.7 0.0 copy-done.4
  20.7 8.4 %shard_map.100.part_ref = f32[2,10,400,128]{3,2,1,0:T(8,128)} custom-call(f32[32]{0:T(128)} %pad_maximum_fusion.1.sc_ref, s32[2]{0:T(128)} %bitcast.29, bf16[20,400,128]{2,1,0:T(8,128)(2,1)} %bitcast.24, bf16[20,400,128]{2,1,0:T(8,128)(2,1)} %bitcast.25, bf16[20,2,200,128]{3,2,1,0:T(8,128)(2,1)} %constant.141.clone.rec_lo.rec_hi.rec_ref, ...), custom_call_target="tpu_custom_call" | custom-call | tf_op jit(solution)/shard_map/pallas_call | solution.py:242
  29.1 6.2 %collective-permute-done.6.pp_ref = f32[16,128]{1,0:T(8,128)S(1)} collective-permute-done((f32[16,128]{1,0:T(8,128)S(1)}, f32[16,128]{1,0:T(8,128)S(1)}, u32[]{:S(2)}, u32[]{:S(2)}) %collective-permute-start.6) | collective-permute-done | bytes 8224 | tf_op jit(solution)/shard_map/ppermute | solution.py:21
  35.3 0.0 copy-start.5
  35.3 3.2 %collective-permute-done.5.pn_ref = f32[16,128]{1,0:T(8,128)S(1)} collective-permute-done((f32[16,128]{1,0:T(8,128)S(1)}, f32[16,128]{1,0:T(8,128)S(1)}, u32[]{:S(2)}, u32[]{:S(2)}) %collective-permute-start.5) | collective-permute-done | bytes 8224 | tf_op jit(solution)/shard_map/ppermute | solution.py:21
  38.5 0.0 copy-start.6
  38.5 0.0 collective-permute-done.4.prv_ref
  38.5 0.0 copy-start.1
  38.5 0.0 collective-permute-done.3.nxt_ref
  38.5 0.0 copy-done.5
  38.5 0.6 %copy-done.6 = f32[16,128]{1,0:T(8,128)} copy-done((f32[16,128]{1,0:T(8,128)}, f32[16,128]{1,0:T(8,128)S(1)}, u32[]{:S(2)}) %copy-start.6) | copy-done | bytes 8216
  39.1 0.4 copy-done.1
  39.5 0.0 copy-start.2
  39.5 1.0 %copy-done.2 = bf16[20,200,128]{2,1,0:T(8,128)(2,1)} copy-done((bf16[20,200,128]{2,1,0:T(8,128)(2,1)}, bf16[20,200,128]{2,1,0:T(8,128)(2,1)S(1)}, u32[]{:S(2)}) %copy-start.2) | copy-done | bytes 1024024
  40.4 7.5 %shard_map.101 = bf16[20,400,128]{2,1,0:T(8,128)(2,1)} custom-call(f32[32]{0:T(128)} %pad_maximum_fusion.1.sc_ref, f32[2,10,400,128]{3,2,1,0:T(8,128)} %shard_map.100.part_ref, bf16[20,200,128]{2,1,0:T(8,128)(2,1)} %copy-done.2, bf16[20,200,128]{2,1,0:T(8,128)(2,1)} %copy-done.1, bf16[20,2,200,128]{3,2,1,0:T(8,128)(2,1)} %constant.141.clone.rec_lo.rec_hi.rec_ref, ...), custom_call_target="tpu_custom_call" | custom-call | tf_op jit(solution)/shard_map/pallas_call | solution.py:315
  (6 shorter events, 0.0 us)
Async XLA Ops:
  1.5 1.8 %copy-start.3 = (bf16[39,8000]{1,0:T(8,128)(2,1)S(1)}, bf16[39,8000]{1,0:T(8,128)(2,1)}, u32[]{:S(2)}) copy-start(bf16[39,8000]{1,0:T(8,128)(2,1)} %constant.139.clone) | copy-start | bytes 1872004
  3.3 7.0 %copy-start = (bf16[1,400,20,128]{3,1,2,0:T(8,128)(2,1)S(1)}, bf16[1,400,20,128]{3,1,2,0:T(8,128)(2,1)}, u32[]{:S(2)}) copy-start(bf16[1,400,20,128]{3,1,2,0:T(8,128)(2,1)} %param.10) | copy-start | bytes 6144004
  3.8 13.4 %collective-permute-start.1 = (f32[13,128]{1,0:T(8,128)S(1)}, f32[13,128]{1,0:T(8,128)S(1)}, u32[]{:S(2)}, u32[]{:S(2)}) collective-permute-start(f32[13,128]{1,0:T(8,128)S(1)} %slice_add_fusion), channel_id=1, source_target_pairs={{0,2},{1,3},{2,0},{3,1},{4,6},{5,7},{6,4},{7,5},{8,10},{9,11},{10,... | collective-permute-start | bytes 19976 | tf_op jit(solution)/shard_map/ppermute | solution.py:21
  7.0 10.2 %collective-permute-start = (f32[13,128]{1,0:T(8,128)S(1)}, f32[13,128]{1,0:T(8,128)S(1)}, u32[]{:S(2)}, u32[]{:S(2)}) collective-permute-start(f32[13,128]{1,0:T(8,128)S(1)} %slice_add_fusion), channel_id=1, source_target_pairs={{0,1},{1,2},{2,3},{3,0},{4,5},{5,6},{6,7},{7,4},{8,9},{9,10},{10,1... | collective-permute-start | bytes 19976 | tf_op jit(solution)/shard_map/ppermute | solution.py:21
  8.3 9.0 %collective-permute-start.2 = (f32[13,128]{1,0:T(8,128)S(1)}, f32[13,128]{1,0:T(8,128)S(1)}, u32[]{:S(2)}, u32[]{:S(2)}) collective-permute-start(f32[13,128]{1,0:T(8,128)S(1)} %slice_add_fusion), channel_id=1, source_target_pairs={{0,3},{1,0},{2,1},{3,2},{4,7},{5,4},{6,5},{7,6},{8,11},{9,8},{10,9... | collective-permute-start | bytes 19976 | tf_op jit(solution)/shard_map/ppermute | solution.py:21
  10.3 4.4 %copy-start.7 = (f32[20]{0:T(128)S(1)}, f32[20]{0:T(128)}, u32[]{:S(2)}) copy-start(f32[20]{0:T(128)} %constant.140.clone) | copy-start | bytes 244
  11.4 27.1 %collective-permute-start.4 = (bf16[20,200,128]{2,1,0:T(8,128)(2,1)}, bf16[20,200,128]{2,1,0:T(8,128)(2,1)S(1)}, u32[]{:S(2)}, u32[]{:S(2)}) collective-permute-start(bf16[20,200,128]{2,1,0:T(8,128)(2,1)} %get-tuple-element.5), channel_id=1, source_target_pairs={{0,4},{4,8},{8,12},{12,16},{16,20},{20,24},{24,28},{28,0},{1,5},{5... | collective-permute-start | bytes 3072008 | tf_op jit(solution)/shard_map/ppermute | solution.py:21
  14.0 24.5 %collective-permute-start.3 = (bf16[20,200,128]{2,1,0:T(8,128)(2,1)S(1)}, bf16[20,200,128]{2,1,0:T(8,128)(2,1)S(1)}, u32[]{:S(2)}, u32[]{:S(2)}) collective-permute-start(bf16[20,200,128]{2,1,0:T(8,128)(2,1)S(1)} %get-tuple-element.6), channel_id=1, source_target_pairs={{0,28},{4,0},{8,4},{12,8},{16,12},{20,16},{24,20},{28,24},{1,29},{... | collective-permute-start | bytes 3072008 | tf_op jit(solution)/shard_map/ppermute | solution.py:21
  17.4 3.3 %copy-start.4 = (f32[16,128]{1,0:T(8,128)}, f32[16,128]{1,0:T(8,128)S(1)}, u32[]{:S(2)}) copy-start(f32[16,128]{1,0:T(8,128)S(1)} %maximum_maximum_fusion.pk_ref) | copy-start | bytes 24580
  17.4 17.9 %collective-permute-start.6 = (f32[16,128]{1,0:T(8,128)S(1)}, f32[16,128]{1,0:T(8,128)S(1)}, u32[]{:S(2)}, u32[]{:S(2)}) collective-permute-start(f32[16,128]{1,0:T(8,128)S(1)} %maximum_maximum_fusion.pk_ref), channel_id=1, source_target_pairs={{0,4},{4,8},{8,12},{12,16},{16,20},{20,24},{24,28},{28,0},{1,5},{5... | collective-permute-start | bytes 24584 | tf_op jit(solution)/shard_map/ppermute | solution.py:21
  19.2 19.3 %collective-permute-start.5 = (f32[16,128]{1,0:T(8,128)S(1)}, f32[16,128]{1,0:T(8,128)S(1)}, u32[]{:S(2)}, u32[]{:S(2)}) collective-permute-start(f32[16,128]{1,0:T(8,128)S(1)} %maximum_maximum_fusion.pk_ref), channel_id=1, source_target_pairs={{0,28},{4,0},{8,4},{12,8},{16,12},{20,16},{24,20},{28,24},{1,29},{... | collective-permute-start | bytes 24584 | tf_op jit(solution)/shard_map/ppermute | solution.py:21
  35.3 3.2 %copy-start.5 = (f32[16,128]{1,0:T(8,128)}, f32[16,128]{1,0:T(8,128)S(1)}, u32[]{:S(2)}) copy-start(f32[16,128]{1,0:T(8,128)S(1)} %collective-permute-done.6.pp_ref) | copy-start | bytes 24580
  38.5 0.6 %copy-start.6 = (f32[16,128]{1,0:T(8,128)}, f32[16,128]{1,0:T(8,128)S(1)}, u32[]{:S(2)}) copy-start(f32[16,128]{1,0:T(8,128)S(1)} %collective-permute-done.5.pn_ref) | copy-start | bytes 24580
  38.5 1.0 %copy-start.1 = (bf16[20,200,128]{2,1,0:T(8,128)(2,1)}, bf16[20,200,128]{2,1,0:T(8,128)(2,1)S(1)}, u32[]{:S(2)}) copy-start(bf16[20,200,128]{2,1,0:T(8,128)(2,1)S(1)} %collective-permute-done.4.prv_ref) | copy-start | bytes 3072004
  39.5 1.0 %copy-start.2 = (bf16[20,200,128]{2,1,0:T(8,128)(2,1)}, bf16[20,200,128]{2,1,0:T(8,128)(2,1)S(1)}, u32[]{:S(2)}) copy-start(bf16[20,200,128]{2,1,0:T(8,128)(2,1)S(1)} %collective-permute-done.3.nxt_ref) | copy-start | bytes 3072004
where the time goes:
time: 48.3 us; the launch traced here: 48 us
  Pallas kernels  15.9 us (33%)
  starting transfers between devices  10.8 us (22%)
  waiting for transfers between devices  9.4 us (19%)
  local copies, waits for them, and re-layouts  5.07 us (10%)
  other arithmetic  4.86 us (10%)
  between operations  1.42 us (3%)
  matrix products  0.5 us (1%)
    ppermute x7, starting transfers between devices, passed_along(): return lax.ppermute(value, axis, pairs)  10.8 us
    ppermute x7, waiting for transfers between devices, passed_along(): return lax.ppermute(value, axis, pairs)  9.4 us
    pallas_call x1, Pallas kernels, own_kernel(): pl.pallas_call(kernel, grid=(blocks,), in_specs=in_specs, out_specs=pl.Bl...  8.38 us
    pallas_call x1, Pallas kernels, halo_kernel(): pl.pallas_call(kernel, grid=(blocks,), in_specs=in_specs, out_specs=pl.Bl...  7.53 us
    unnamed x16, local copies, waits for them, and re-layouts  1.95 us
    mul x1, other arithmetic, on_device(): masked = field_in * keep.astype(jnp.bfloat16)  1.81 us
    slice x1, local copies, waits for them, and re-layouts, on_device(): lower_in = field_in[:, :half, :]  1.1 us
  transfers between devices with their start and end apart: 7, of which 2 were waited for; matrix products, arithmetic and copies ran while one was open for 10% of the time, Pallas kernels for 17%

commit v1 on v0

--- a/solution.py
+++ b/solution.py
@@ -153,25 +153,26 @@
     moment_count, pair_count, node_count = recon.shape
     half = pair_count // 2
     table = np.transpose(recon, (2, 1, 0))
-    parts = bf16_split(table, 3)
-    order = [0, 0, 1, 0, 1, 2]
-    packed = np.zeros((node_count, pair_count, lanes), np.float32)
-    for block, part in enumerate(order):
-        packed[:, :, block * rows : block * rows + moment_count] = parts[part]
-    packed = packed.reshape(node_count, 2, half, lanes)
+    parts = bf16_split(table, 2)
+    order = [0, 0, 1]
+    packed = np.zeros((node_count, half, lanes), np.float32)
+    for side in range(2):
+        for block, part in enumerate(order):
+            at = side * (lanes // 2) + block * rows
+            packed[:, :, at : at + moment_count] = parts[part][:, side * half : (side + 1) * half]
     return packed.astype(jnp.bfloat16)
 
 
-def cross_matrix(packet, moment_count):
-    rows = packet.shape[0]
+def cross_matrix(packet, moment_count, side):
+    rows, cells = packet.shape
     row = lax.broadcasted_iota(jnp.int32, packet.shape, 0)
     values = jnp.where(row < moment_count, packet, 0.0)
     c1 = values.astype(jnp.bfloat16)
-    left = values - c1.astype(jnp.float32)
-    c2 = left.astype(jnp.bfloat16)
-    c3 = (left - c2.astype(jnp.float32)).astype(jnp.bfloat16)
-    pad = jnp.zeros((128 - 6 * rows, packet.shape[1]), jnp.bfloat16)
-    return jnp.concatenate([c1, c2, c1, c3, c2, c1, pad], axis=0)
+    c2 = (values - c1.astype(jnp.float32)).astype(jnp.bfloat16)
+    gap = jnp.zeros((64 - 3 * rows, cells), jnp.bfloat16)
+    lead = jnp.zeros((64, cells), jnp.bfloat16)
+    pieces = [c1, c2, c1, gap]
+    return jnp.concatenate([lead] + pieces if side else pieces + [lead], axis=0)
 
 
 def own_kernel(field_in, recon_halves, packet, columns, flip, scalars, faces):
@@ -189,16 +190,18 @@
         pk = pk_ref[...]
         rate = sc_ref[31]
         keep = rate * jnp.where(row >= half, pk[moment_count + 1 : moment_count + 2, :], pk[moment_count : moment_count + 1, :])
-        own = cross_matrix(pk, moment_count)
+        own_lo = cross_matrix(pk, moment_count, 0)
+        own_hi = cross_matrix(pk, moment_count, 1)
         base = col_ref[0]
         face_a = face_ref[0] == 1
         face_b = face_ref[1] == 1
 
         def relax(values, rec_ref, at):
+            rec = rec_ref[at]
             rebuilt = jnp.concatenate(
                 [
-                    jnp.dot(rec_ref[at, 0], own, preferred_element_type=jnp.float32),
-                    jnp.dot(rec_ref[at, 1], own, preferred_element_type=jnp.float32),
+                    jnp.dot(rec, own_lo, preferred_element_type=jnp.float32),
+                    jnp.dot(rec, own_hi, preferred_element_type=jnp.float32),
                 ],
                 axis=0,
             )
@@ -233,8 +236,8 @@
         smem,
         pl.BlockSpec(block, lambda b: (b, 0, 0)),
         pl.BlockSpec(block, lambda b: (2 * blocks - 1 - b, 0, 0)),
-        pl.BlockSpec((group, 2, half, recon_halves.shape[3]), lambda b: (b, 0, 0, 0)),
-        pl.BlockSpec((group, 2, half, recon_halves.shape[3]), lambda b: (2 * blocks - 1 - b, 0, 0, 0)),
+        pl.BlockSpec((group, half, recon_halves.shape[2]), lambda b: (b, 0, 0)),
+        pl.BlockSpec((group, half, recon_halves.shape[2]), lambda b: (2 * blocks - 1 - b, 0, 0)),
         pl.BlockSpec(packet.shape, lambda b: (0, 0)),
         pl.BlockSpec((1, pair_count, cell_count), lambda b: (0, 0, 0)),
         pl.BlockSpec(flip.shape, lambda b: (0, 0)),
@@ -265,16 +268,17 @@
         rate = sc_ref[31]
         pn = pn_ref[...]
         pp = pp_ref[...]
-        next_mat = cross_matrix(pn, moment_count)
-        prev_mat = cross_matrix(pp, moment_count)
+        next_mat = cross_matrix(pn, moment_count, 1)
+        prev_mat = cross_matrix(pp, moment_count, 0)
         keep_up = rate * pn[moment_count + 1 : moment_count + 2, :]
         keep_down = rate * pp[moment_count : moment_count + 1, :]
         side = col_ref[0]
 
         def run(mirrored):
             def one(t, carry):
-                up = jnp.dot(rec_ref[t, 1], next_mat, preferred_element_type=jnp.float32)
-                down = jnp.dot(rec_ref[t, 0], prev_mat, preferred_element_type=jnp.float32)
+                rec = rec_ref[t]
+                up = jnp.dot(rec, next_mat, preferred_element_type=jnp.float32)
+                down = jnp.dot(rec, prev_mat, preferred_element_type=jnp.float32)
                 up = (keep_up * nxt_ref[t].astype(jnp.float32) + up).astype(jnp.bfloat16)
                 down = (keep_down * prv_ref[t].astype(jnp.float32) + down).astype(jnp.bfloat16)
                 shifted = jnp.concatenate([down.astype(jnp.float32), up.astype(jnp.float32)], axis=0)
@@ -307,7 +311,7 @@
         ),
         pl.BlockSpec((group, half, cell_count), lambda i: (i, 0, 0)),
         pl.BlockSpec((group, half, cell_count), lambda i: (i, 0, 0)),
-        pl.BlockSpec((group, 2, half, recon_halves.shape[3]), lambda i: (i, 0, 0, 0)),
+        pl.BlockSpec((group, half, recon_halves.shape[2]), lambda i: (i, 0, 0)),
         pl.BlockSpec(packet_next.shape, lambda i: (0, 0)),
         pl.BlockSpec(packet_prev.shape, lambda i: (0, 0)),
         pl.BlockSpec((1, pair_count, cell_count), lambda i: (1, 0, 0)),

time: 48.3 us -> 48 us (level)
  no operation moved by 1% of the time
where the time goes in v1:
time: 48 us; the launch traced here: 47.8 us
  Pallas kernels  15.5 us (32%)
  starting transfers between devices  10.8 us (22%)
  waiting for transfers between devices  9.59 us (20%)
  local copies, waits for them, and re-layouts  5.07 us (11%)
  other arithmetic  4.86 us (10%)
  between operations  1.42 us (3%)
  matrix products  0.5 us (1%)
    ppermute x7, starting transfers between devices, passed_along(): return lax.ppermute(value, axis, pairs)  10.8 us
    ppermute x7, waiting for transfers between devices, passed_along(): return lax.ppermute(value, axis, pairs)  9.59 us
    pallas_call x1, Pallas kernels, own_kernel(): pl.pallas_call(kernel, grid=(blocks,), in_specs=in_specs, out_specs=pl.Bl...  8.19 us
    pallas_call x1, Pallas kernels, halo_kernel(): pl.pallas_call(kernel, grid=(blocks,), in_specs=in_specs, out_specs=pl.Bl...  7.31 us
    unnamed x16, local copies, waits for them, and re-layouts  1.95 us
    mul x1, other arithmetic, on_device(): masked = field_in * keep.astype(jnp.bfloat16)  1.81 us
    slice x1, local copies, waits for them, and re-layouts, on_device(): lower_in = field_in[:, :half, :]  1.1 us
  transfers between devices with their start and end apart: 7, of which 2 were waited for; matrix products, arithmetic and copies ran while one was open for 10% of the time, Pallas kernels for 17%

profile of v1, /device:TPU:1, one launch (start us, length us, event | category | flops | bytes accessed | tf_op | source)
XLA Modules:
  0.0 47.8 jit_solution(11493830514778259526)
XLA Ops:
  0.0 0.7 %subtract_convert_fusion = (bf16[128]{0:T(256)(128)(2,1)S(1)}, f32[1,128]{1,0:T(1,128)S(1)}) fusion(s32[128]{0:T(128)} %param.14), kind=kLoop, calls=%fused_computation.21 | loop fusion | flops 384 | bytes 1280 | tf_op jit(solution)/shard_map/convert_element_type | solution.py:87
  0.7 0.7 %subtract_multiply_fusion = f32[128]{0:T(128)S(1)} fusion(s32[128]{0:T(128)} %param.15, s32[128]{0:T(128)} %param.14), kind=kLoop, calls=%fused_computation.20 | loop fusion | flops 640 | bytes 1536 | tf_op jit(solution)/shard_map/mul | solution.py:88
  1.3 0.1 select_convert_fusion
  1.5 0.0 copy-start.3
  1.5 1.8 %broadcast_multiply_fusion = bf16[20,400,128]{2,1,0:T(8,128)(2,1)S(1)} fusion(bf16[400,128]{1,0:T(8,128)(2,1)S(1)} %select_convert_fusion, bf16[1,400,20,128]{3,1,2,0:T(8,128)(2,1)} %param.10), kind=kLoop, calls=%fused_computation | loop fusion | flops 1024000 | bytes 4198400 | tf_op jit(solution)/shard_map/mul | solution.py:91
  3.3 0.0 copy-start
  3.3 0.0 copy-done.3
  3.3 0.5 %fusion.7 = f32[39,128]{1,0:T(8,128)S(1)} fusion(bf16[39,8000]{1,0:T(8,128)(2,1)S(1)} %copy-done.3, bf16[8000,128]{1,0:T(8,128)(2,1)S(1)} %bitcast.27), kind=kOutput, calls=%fused_computation.25 | convolution fusion | flops 79872000 | bytes 2691968 | tf_op jit(solution)/shard_map/dot_general | solution.py:92
  3.8 3.2 %collective-permute-start.1 = (f32[13,128]{1,0:T(8,128)S(1)}, f32[13,128]{1,0:T(8,128)S(1)}, u32[]{:S(2)}, u32[]{:S(2)}) collective-permute-start(f32[13,128]{1,0:T(8,128)S(1)} %slice_add_fusion), channel_id=1, source_target_pairs={{0,2},{1,3},{2,0},{3,1},{4,6},{5,7},{6,4},{7,5},{8,10},{9,11},{10,... | collective-permute-start | bytes 19976 | tf_op jit(solution)/shard_map/ppermute | solution.py:21
  7.0 1.3 %collective-permute-start = (f32[13,128]{1,0:T(8,128)S(1)}, f32[13,128]{1,0:T(8,128)S(1)}, u32[]{:S(2)}, u32[]{:S(2)}) collective-permute-start(f32[13,128]{1,0:T(8,128)S(1)} %slice_add_fusion), channel_id=1, source_target_pairs={{0,1},{1,2},{2,3},{3,0},{4,5},{5,6},{6,7},{7,4},{8,9},{9,10},{10,1... | collective-permute-start | bytes 19976 | tf_op jit(solution)/shard_map/ppermute | solution.py:21
  8.3 2.0 %collective-permute-start.2 = (f32[13,128]{1,0:T(8,128)S(1)}, f32[13,128]{1,0:T(8,128)S(1)}, u32[]{:S(2)}, u32[]{:S(2)}) collective-permute-start(f32[13,128]{1,0:T(8,128)S(1)} %slice_add_fusion), channel_id=1, source_target_pairs={{0,3},{1,0},{2,1},{3,2},{4,7},{5,4},{6,5},{7,6},{8,11},{9,8},{10,9... | collective-permute-start | bytes 19976 | tf_op jit(solution)/shard_map/ppermute | solution.py:21
  10.3 0.0 copy-done
  10.3 0.0 copy-start.7
  10.3 1.1 %fusion.6 = (bf16[20,200,128]{2,1,0:T(8,128)(2,1)}, bf16[20,200,128]{2,1,0:T(8,128)(2,1)S(1)}) fusion(bf16[20,400,128]{2,1,0:T(8,128)(2,1)S(1)} %bitcast.26), kind=kLoop, calls=%fused_computation.24 | loop fusion | bytes 4096000 | tf_op jit(solution)/shard_map/slice | solution.py:83
  11.4 2.6 %collective-permute-start.4 = (bf16[20,200,128]{2,1,0:T(8,128)(2,1)}, bf16[20,200,128]{2,1,0:T(8,128)(2,1)S(1)}, u32[]{:S(2)}, u32[]{:S(2)}) collective-permute-start(bf16[20,200,128]{2,1,0:T(8,128)(2,1)} %get-tuple-element.5), channel_id=1, source_target_pairs={{0,4},{4,8},{8,12},{12,16},{16,20},{20,24},{24,28},{28,0},{1,5},{5... | collective-permute-start | bytes 3072008 | tf_op jit(solution)/shard_map/ppermute | solution.py:21
  14.0 0.0 collective-permute-start.3
  14.7 0.0 copy-done.7
  14.7 0.1 broadcast_in_dim.59
  14.8 0.1 abs.20
  14.9 0.8 %fusion.flip_ref = bf16[400,400]{1,0:T(8,128)(2,1)} fusion(), kind=kLoop, calls=%fused_computation.2 | loop fusion | flops 480000 | bytes 320000 | tf_op jit(solution)/shard_map/convert_element_type | solution.py:142
  15.7 0.8 %fusion.1 = (f32[13]{0:T(128)S(1)}, f32[13]{0:T(128)S(1)}, f32[13]{0:T(128)S(1)}, f32[13]{0:T(128)S(1)}) fusion(f32[4,4,13]{2,1,0:T(4,128)} %param.13, s32[]{:T(128)S(6)} %select_n.48, s32[]{:T(128)S(6)} %select_n.52, s32[]{:T(128)S(6)} %select_n.58, s32[]{:T(128)S(6)} %select_n.55), kind=kLoop, calls=%fused_computation.15 | loop fusion | bytes 432 | tf_op jit(solution)/shard_map/mul | solution.py:102
  17.2 0.1 pad.5.clone
  17.3 0.0 collective-permute-done.1
  17.3 0.0 collective-permute-done
  17.3 0.0 collective-permute-done.2
  17.3 0.1 multiply_add_fusion
  17.4 0.1 maximum_maximum_fusion.pk_ref
  17.4 0.0 copy-start.4
  17.4 1.7 %collective-permute-start.6 = (f32[16,128]{1,0:T(8,128)S(1)}, f32[16,128]{1,0:T(8,128)S(1)}, u32[]{:S(2)}, u32[]{:S(2)}) collective-permute-start(f32[16,128]{1,0:T(8,128)S(1)} %maximum_maximum_fusion.pk_ref), channel_id=1, source_target_pairs={{0,4},{4,8},{8,12},{12,16},{16,20},{20,24},{24,28},{28,0},{1,5},{5... | collective-permute-start | bytes 24584 | tf_op jit(solution)/shard_map/ppermute | solution.py:21
  19.2 0.0 collective-permute-start.5
  19.2 0.6 %pad_maximum_fusion.1.sc_ref = f32[32]{0:T(128)} fusion(f32[1]{0:T(128)S(6)} %sub.38, f32[11]{0:T(128)S(1)} %broadcast.71, f32[20]{0:T(128)S(1)} %multiply_abs_fusion), kind=kLoop, calls=%fused_computation.19 | loop fusion | flops 64 | bytes 256 | tf_op jit(solution)/shard_map/concatenate | solution.py:132
  19.8 0.9 %broadcast_in_dim.60.col_ref = f32[2,400,128]{2,1,0:T(8,128)} broadcast(f32[2,400]{1,0:T(2,128)S(1)} %pad_maximum_fusion), dimensions={0,1} | broadcast | bytes 412800 | tf_op jit(solution)/shard_map/broadcast_in_dim | solution.py:129
  20.7 0.0 copy-done.4
  20.7 8.2 %shard_map.100.part_ref = f32[2,10,400,128]{3,2,1,0:T(8,128)} custom-call(f32[32]{0:T(128)} %pad_maximum_fusion.1.sc_ref, s32[2]{0:T(128)} %bitcast.29, bf16[20,400,128]{2,1,0:T(8,128)(2,1)} %bitcast.24, bf16[20,400,128]{2,1,0:T(8,128)(2,1)} %bitcast.25, bf16[20,200,128]{2,1,0:T(8,128)(2,1)} %constant.141.clone.rec_lo.rec_hi.rec_ref, ...), custom_call_target="tpu_custom_call" | custom-call | tf_op jit(solution)/shard_map/pallas_call | solution.py:245
  28.9 6.4 %collective-permute-done.6.pp_ref = f32[16,128]{1,0:T(8,128)S(1)} collective-permute-done((f32[16,128]{1,0:T(8,128)S(1)}, f32[16,128]{1,0:T(8,128)S(1)}, u32[]{:S(2)}, u32[]{:S(2)}) %collective-permute-start.6) | collective-permute-done | bytes 8224 | tf_op jit(solution)/shard_map/ppermute | solution.py:21
  35.3 0.0 copy-start.5
  35.3 3.2 %collective-permute-done.5.pn_ref = f32[16,128]{1,0:T(8,128)S(1)} collective-permute-done((f32[16,128]{1,0:T(8,128)S(1)}, f32[16,128]{1,0:T(8,128)S(1)}, u32[]{:S(2)}, u32[]{:S(2)}) %collective-permute-start.5) | collective-permute-done | bytes 8224 | tf_op jit(solution)/shard_map/ppermute | solution.py:21
  38.5 0.0 copy-start.6
  38.5 0.0 collective-permute-done.4.prv_ref
  38.5 0.0 copy-start.1
  38.5 0.0 collective-permute-done.3.nxt_ref
  38.5 0.0 copy-done.5
  38.5 0.6 %copy-done.6 = f32[16,128]{1,0:T(8,128)} copy-done((f32[16,128]{1,0:T(8,128)}, f32[16,128]{1,0:T(8,128)S(1)}, u32[]{:S(2)}) %copy-start.6) | copy-done | bytes 8216
  39.1 0.4 copy-done.1
  39.5 0.0 copy-start.2
  39.5 1.0 %copy-done.2 = bf16[20,200,128]{2,1,0:T(8,128)(2,1)} copy-done((bf16[20,200,128]{2,1,0:T(8,128)(2,1)}, bf16[20,200,128]{2,1,0:T(8,128)(2,1)S(1)}, u32[]{:S(2)}) %copy-start.2) | copy-done | bytes 1024024
  40.4 7.3 %shard_map.101 = bf16[20,400,128]{2,1,0:T(8,128)(2,1)} custom-call(f32[32]{0:T(128)} %pad_maximum_fusion.1.sc_ref, f32[2,10,400,128]{3,2,1,0:T(8,128)} %shard_map.100.part_ref, bf16[20,200,128]{2,1,0:T(8,128)(2,1)} %copy-done.2, bf16[20,200,128]{2,1,0:T(8,128)(2,1)} %copy-done.1, bf16[20,200,128]{2,1,0:T(8,128)(2,1)} %constant.141.clone.rec_lo.rec_hi.rec_ref, ...), custom_call_target="tpu_custom_call" | custom-call | tf_op jit(solution)/shard_map/pallas_call | solution.py:319
  (6 shorter events, 0.0 us)
Async XLA Ops:
  1.5 1.8 %copy-start.3 = (bf16[39,8000]{1,0:T(8,128)(2,1)S(1)}, bf16[39,8000]{1,0:T(8,128)(2,1)}, u32[]{:S(2)}) copy-start(bf16[39,8000]{1,0:T(8,128)(2,1)} %constant.139.clone) | copy-start | bytes 1872004
  3.3 7.0 %copy-start = (bf16[1,400,20,128]{3,1,2,0:T(8,128)(2,1)S(1)}, bf16[1,400,20,128]{3,1,2,0:T(8,128)(2,1)}, u32[]{:S(2)}) copy-start(bf16[1,400,20,128]{3,1,2,0:T(8,128)(2,1)} %param.10) | copy-start | bytes 6144004
  3.8 13.4 %collective-permute-start.1 = (f32[13,128]{1,0:T(8,128)S(1)}, f32[13,128]{1,0:T(8,128)S(1)}, u32[]{:S(2)}, u32[]{:S(2)}) collective-permute-start(f32[13,128]{1,0:T(8,128)S(1)} %slice_add_fusion), channel_id=1, source_target_pairs={{0,2},{1,3},{2,0},{3,1},{4,6},{5,7},{6,4},{7,5},{8,10},{9,11},{10,... | collective-permute-start | bytes 19976 | tf_op jit(solution)/shard_map/ppermute | solution.py:21
  7.0 10.2 %collective-permute-start = (f32[13,128]{1,0:T(8,128)S(1)}, f32[13,128]{1,0:T(8,128)S(1)}, u32[]{:S(2)}, u32[]{:S(2)}) collective-permute-start(f32[13,128]{1,0:T(8,128)S(1)} %slice_add_fusion), channel_id=1, source_target_pairs={{0,1},{1,2},{2,3},{3,0},{4,5},{5,6},{6,7},{7,4},{8,9},{9,10},{10,1... | collective-permute-start | bytes 19976 | tf_op jit(solution)/shard_map/ppermute | solution.py:21
  8.3 9.0 %collective-permute-start.2 = (f32[13,128]{1,0:T(8,128)S(1)}, f32[13,128]{1,0:T(8,128)S(1)}, u32[]{:S(2)}, u32[]{:S(2)}) collective-permute-start(f32[13,128]{1,0:T(8,128)S(1)} %slice_add_fusion), channel_id=1, source_target_pairs={{0,3},{1,0},{2,1},{3,2},{4,7},{5,4},{6,5},{7,6},{8,11},{9,8},{10,9... | collective-permute-start | bytes 19976 | tf_op jit(solution)/shard_map/ppermute | solution.py:21
  10.3 4.4 %copy-start.7 = (f32[20]{0:T(128)S(1)}, f32[20]{0:T(128)}, u32[]{:S(2)}) copy-start(f32[20]{0:T(128)} %constant.140.clone) | copy-start | bytes 244
  11.4 27.1 %collective-permute-start.4 = (bf16[20,200,128]{2,1,0:T(8,128)(2,1)}, bf16[20,200,128]{2,1,0:T(8,128)(2,1)S(1)}, u32[]{:S(2)}, u32[]{:S(2)}) collective-permute-start(bf16[20,200,128]{2,1,0:T(8,128)(2,1)} %get-tuple-element.5), channel_id=1, source_target_pairs={{0,4},{4,8},{8,12},{12,16},{16,20},{20,24},{24,28},{28,0},{1,5},{5... | collective-permute-start | bytes 3072008 | tf_op jit(solution)/shard_map/ppermute | solution.py:21
  14.0 24.5 %collective-permute-start.3 = (bf16[20,200,128]{2,1,0:T(8,128)(2,1)S(1)}, bf16[20,200,128]{2,1,0:T(8,128)(2,1)S(1)}, u32[]{:S(2)}, u32[]{:S(2)}) collective-permute-start(bf16[20,200,128]{2,1,0:T(8,128)(2,1)S(1)} %get-tuple-element.6), channel_id=1, source_target_pairs={{0,28},{4,0},{8,4},{12,8},{16,12},{20,16},{24,20},{28,24},{1,29},{... | collective-permute-start | bytes 3072008 | tf_op jit(solution)/shard_map/ppermute | solution.py:21
  17.4 3.3 %copy-start.4 = (f32[16,128]{1,0:T(8,128)}, f32[16,128]{1,0:T(8,128)S(1)}, u32[]{:S(2)}) copy-start(f32[16,128]{1,0:T(8,128)S(1)} %maximum_maximum_fusion.pk_ref) | copy-start | bytes 24580
  17.4 17.9 %collective-permute-start.6 = (f32[16,128]{1,0:T(8,128)S(1)}, f32[16,128]{1,0:T(8,128)S(1)}, u32[]{:S(2)}, u32[]{:S(2)}) collective-permute-start(f32[16,128]{1,0:T(8,128)S(1)} %maximum_maximum_fusion.pk_ref), channel_id=1, source_target_pairs={{0,4},{4,8},{8,12},{12,16},{16,20},{20,24},{24,28},{28,0},{1,5},{5... | collective-permute-start | bytes 24584 | tf_op jit(solution)/shard_map/ppermute | solution.py:21
  19.2 19.3 %collective-permute-start.5 = (f32[16,128]{1,0:T(8,128)S(1)}, f32[16,128]{1,0:T(8,128)S(1)}, u32[]{:S(2)}, u32[]{:S(2)}) collective-permute-start(f32[16,128]{1,0:T(8,128)S(1)} %maximum_maximum_fusion.pk_ref), channel_id=1, source_target_pairs={{0,28},{4,0},{8,4},{12,8},{16,12},{20,16},{24,20},{28,24},{1,29},{... | collective-permute-start | bytes 24584 | tf_op jit(solution)/shard_map/ppermute | solution.py:21
  35.3 3.2 %copy-start.5 = (f32[16,128]{1,0:T(8,128)}, f32[16,128]{1,0:T(8,128)S(1)}, u32[]{:S(2)}) copy-start(f32[16,128]{1,0:T(8,128)S(1)} %collective-permute-done.6.pp_ref) | copy-start | bytes 24580
  38.5 0.6 %copy-start.6 = (f32[16,128]{1,0:T(8,128)}, f32[16,128]{1,0:T(8,128)S(1)}, u32[]{:S(2)}) copy-start(f32[16,128]{1,0:T(8,128)S(1)} %collective-permute-done.5.pn_ref) | copy-start | bytes 24580
  38.5 1.0 %copy-start.1 = (bf16[20,200,128]{2,1,0:T(8,128)(2,1)}, bf16[20,200,128]{2,1,0:T(8,128)(2,1)S(1)}, u32[]{:S(2)}) copy-start(bf16[20,200,128]{2,1,0:T(8,128)(2,1)S(1)} %collective-permute-done.4.prv_ref) | copy-start | bytes 3072004
  39.5 1.0 %copy-start.2 = (bf16[20,200,128]{2,1,0:T(8,128)(2,1)}, bf16[20,200,128]{2,1,0:T(8,128)(2,1)S(1)}, u32[]{:S(2)}) copy-start(bf16[20,200,128]{2,1,0:T(8,128)(2,1)S(1)} %collective-permute-done.3.nxt_ref) | copy-start | bytes 3072004

commit v2 on v1

--- a/solution.py
+++ b/solution.py
@@ -79,8 +79,8 @@
     weight_k = (recon[0] / basis[0]).T.reshape(-1).astype(np.float32)
 
     field_in = jnp.transpose(cotangent[0], (1, 0, 2))
-    upper_in = field_in[:, half:, :]
-    lower_in = field_in[:, :half, :]
+    margin = (-half) % 16
+    upper_in, lower_in = split_halves(field_in, half - margin, half + margin)
     got_next = passed_along(upper_in, "space", -1)
     got_prev = passed_along(lower_in, "space", 1)
 
@@ -161,6 +161,28 @@
             at = side * (lanes // 2) + block * rows
             packed[:, :, at : at + moment_count] = parts[part][:, side * half : (side + 1) * half]
     return packed.astype(jnp.bfloat16)
+
+
+def split_halves(field_in, start, wide):
+    node_count, _, cell_count = field_in.shape
+
+    def kernel(x_hbm, up_hbm, lo_hbm, sems):
+        up = pltpu.make_async_copy(x_hbm.at[:, pl.ds(start, wide), :], up_hbm, sems.at[0])
+        lo = pltpu.make_async_copy(x_hbm.at[:, pl.ds(0, wide), :], lo_hbm, sems.at[1])
+        up.start()
+        lo.start()
+        up.wait()
+        lo.wait()
+
+    shape = jax.ShapeDtypeStruct((node_count, wide, cell_count), field_in.dtype)
+    any_space = pl.BlockSpec(memory_space=pl.ANY)
+    return pl.pallas_call(
+        kernel,
+        in_specs=[any_space],
+        out_specs=[any_space, any_space],
+        out_shape=[shape, shape],
+        scratch_shapes=[pltpu.SemaphoreType.DMA((2,))],
+    )(field_in)
 
 
 def cross_matrix(packet, moment_count, side):
@@ -255,7 +277,9 @@
 
 
 def halo_kernel(partial, got_next, got_prev, recon_halves, packet_next, packet_prev, columns, scalars):
-    node_count, half, cell_count = got_next.shape
+    node_count, wide, cell_count = got_next.shape
+    half = recon_halves.shape[1]
+    margin = wide - half
     pair_count = 2 * half
     steps = node_count // 2
     moment_count = packet_next.shape[0] - 3
@@ -279,8 +303,10 @@
                 rec = rec_ref[t]
                 up = jnp.dot(rec, next_mat, preferred_element_type=jnp.float32)
                 down = jnp.dot(rec, prev_mat, preferred_element_type=jnp.float32)
-                up = (keep_up * nxt_ref[t].astype(jnp.float32) + up).astype(jnp.bfloat16)
-                down = (keep_down * prv_ref[t].astype(jnp.float32) + down).astype(jnp.bfloat16)
+                nxt = nxt_ref[t].astype(jnp.float32)[margin:]
+                prv = prv_ref[t].astype(jnp.float32)[:half]
+                up = (keep_up * nxt + up).astype(jnp.bfloat16)
+                down = (keep_down * prv + down).astype(jnp.bfloat16)
                 shifted = jnp.concatenate([down.astype(jnp.float32), up.astype(jnp.float32)], axis=0)
                 part = part_ref[0, group - 1 - t] if mirrored else part_ref[0, t]
                 out_ref[t] = (part + side * shifted).astype(jnp.bfloat16)
@@ -309,8 +335,8 @@
                 0,
             ),
         ),
-        pl.BlockSpec((group, half, cell_count), lambda i: (i, 0, 0)),
-        pl.BlockSpec((group, half, cell_count), lambda i: (i, 0, 0)),
+        pl.BlockSpec((group, wide, cell_count), lambda i: (i, 0, 0)),
+        pl.BlockSpec((group, wide, cell_count), lambda i: (i, 0, 0)),
         pl.BlockSpec((group, half, recon_halves.shape[2]), lambda i: (i, 0, 0)),
         pl.BlockSpec(packet_next.shape, lambda i: (0, 0)),
         pl.BlockSpec(packet_prev.shape, lambda i: (0, 0)),

time: 48 us -> 114 us (2.38)
  the two profiles are of different devices: /device:TPU:1 before, /device:TPU:0 now
where the time goes in v2:
time: 114 us
  Pallas kernels  81.1 us (71%)
  starting transfers between devices  11.8 us (10%)
  waiting for transfers between devices  10.3 us (9%)
  other arithmetic  4.86 us (4%)
  local copies, waits for them, and re-layouts  3.98 us (3%)
  between operations  1.43 us (1%)
    pallas_call x1, Pallas kernels, split_halves(): pl.pallas_call(kernel, in_specs=[any_space], out_specs=[any_space, any_sp...  65.6 us
    ppermute x7, starting transfers between devices, passed_along(): return lax.ppermute(value, axis, pairs)  11.8 us
    ppermute x7, waiting for transfers between devices, passed_along(): return lax.ppermute(value, axis, pairs)  10.3 us
    pallas_call x1, Pallas kernels, own_kernel(): pl.pallas_call(kernel, grid=(blocks,), in_specs=in_specs, out_specs=pl.Bl...  8.18 us
    pallas_call x1, Pallas kernels, halo_kernel(): pl.pallas_call(kernel, grid=(blocks,), in_specs=in_specs, out_specs=pl.Bl...  7.29 us
  transfers between devices with their start and end apart: 7, of which 1 were waited for; matrix products, arithmetic and copies ran while one was open for 3% of the time, Pallas kernels for 65%

profile of v2, /device:TPU:0, one launch (start us, length us, event | category | flops | bytes accessed | tf_op | source)
XLA Modules:
  0.0 114.0 jit_solution(5962346284382296608)
XLA Ops:
  0.0 0.7 subtract_convert_fusion
  0.7 0.7 subtract_multiply_fusion
  1.3 0.1 select_convert_fusion
  1.5 0.0 copy-start.2
  1.5 1.8 %broadcast_multiply_fusion = bf16[20,400,128]{2,1,0:T(8,128)(2,1)S(1)} fusion(bf16[400,128]{1,0:T(8,128)(2,1)S(1)} %select_convert_fusion, bf16[1,400,20,128]{3,1,2,0:T(8,128)(2,1)} %param.10), kind=kLoop, calls=%fused_computation | loop fusion | flops 1024000 | bytes 4198400 | tf_op jit(solution)/shard_map/mul | solution.py:91
  3.3 0.0 copy-done.2
  3.3 0.0 copy-start.6
  3.3 0.5 fusion.6
  3.8 4.1 %collective-permute-start.1 = (f32[13,128]{1,0:T(8,128)S(1)}, f32[13,128]{1,0:T(8,128)S(1)}, u32[]{:S(2)}, u32[]{:S(2)}) collective-permute-start(f32[13,128]{1,0:T(8,128)S(1)} %slice_add_fusion), channel_id=1, source_target_pairs={{0,2},{1,3},{2,0},{3,1},{4,6},{5,7},{6,4},{7,5},{8,10},{9,11},{10,... | collective-permute-start | bytes 19976 | tf_op jit(solution)/shard_map/ppermute | solution.py:21
  8.0 1.6 %collective-permute-start = (f32[13,128]{1,0:T(8,128)S(1)}, f32[13,128]{1,0:T(8,128)S(1)}, u32[]{:S(2)}, u32[]{:S(2)}) collective-permute-start(f32[13,128]{1,0:T(8,128)S(1)} %slice_add_fusion), channel_id=1, source_target_pairs={{0,1},{1,2},{2,3},{3,0},{4,5},{5,6},{6,7},{7,4},{8,9},{9,10},{10,1... | collective-permute-start | bytes 19976 | tf_op jit(solution)/shard_map/ppermute | solution.py:21
  9.5 2.2 %collective-permute-start.2 = (f32[13,128]{1,0:T(8,128)S(1)}, f32[13,128]{1,0:T(8,128)S(1)}, u32[]{:S(2)}, u32[]{:S(2)}) collective-permute-start(f32[13,128]{1,0:T(8,128)S(1)} %slice_add_fusion), channel_id=1, source_target_pairs={{0,3},{1,0},{2,1},{3,2},{4,7},{5,4},{6,5},{7,6},{8,11},{9,8},{10,9... | collective-permute-start | bytes 19976 | tf_op jit(solution)/shard_map/ppermute | solution.py:21
  11.8 65.6 %shard_map.101 = (bf16[20,208,128]{2,1,0:T(8,128)(2,1)}, bf16[20,208,128]{2,1,0:T(8,128)(2,1)}) custom-call(bf16[20,400,128]{2,1,0:T(8,128)(2,1)} %bitcast.24), custom_call_target="tpu_custom_call" | custom-call | tf_op jit(solution)/shard_map/pallas_call | solution.py:179
  77.4 1.1 collective-permute-start.3
  78.5 0.0 collective-permute-start.4
  79.2 0.0 copy-done.6
  79.2 0.1 broadcast_in_dim.59
  79.3 0.1 abs.20
  79.4 0.8 fusion.flip_ref
  80.2 0.8 fusion.1
  81.7 0.1 pad.5.clone
  81.8 0.0 collective-permute-done.1
  81.8 0.0 collective-permute-done
  81.8 0.0 collective-permute-done.2
  81.8 0.1 multiply_add_fusion
  81.9 0.1 maximum_maximum_fusion.pk_ref
  82.0 0.0 copy-start.3
  82.0 0.6 collective-permute-start.6
  82.6 2.1 %collective-permute-start.5 = (f32[16,128]{1,0:T(8,128)S(1)}, f32[16,128]{1,0:T(8,128)S(1)}, u32[]{:S(2)}, u32[]{:S(2)}) collective-permute-start(f32[16,128]{1,0:T(8,128)S(1)} %maximum_maximum_fusion.pk_ref), channel_id=1, source_target_pairs={{0,28},{4,0},{8,4},{12,8},{16,12},{20,16},{24,20},{28,24},{1,29},{... | collective-permute-start | bytes 24584 | tf_op jit(solution)/shard_map/ppermute | solution.py:21
  84.7 0.6 pad_maximum_fusion.1.sc_ref
  85.3 0.9 broadcast_in_dim.60.col_ref
  86.2 0.0 copy-done.3
  86.2 8.2 %shard_map.100.part_ref = f32[2,10,400,128]{3,2,1,0:T(8,128)} custom-call(f32[32]{0:T(128)} %pad_maximum_fusion.1.sc_ref, s32[2]{0:T(128)} %bitcast.29, bf16[20,400,128]{2,1,0:T(8,128)(2,1)} %bitcast.25, bf16[20,400,128]{2,1,0:T(8,128)(2,1)} %bitcast.26, bf16[20,200,128]{2,1,0:T(8,128)(2,1)} %constant.141.clone.rec_lo.rec_hi.rec_ref, ...), custom_call_target="tpu_custom_call" | custom-call | tf_op jit(solution)/shard_map/pallas_call | solution.py:267
  94.4 10.3 %collective-permute-done.6.pp_ref = f32[16,128]{1,0:T(8,128)S(1)} collective-permute-done((f32[16,128]{1,0:T(8,128)S(1)}, f32[16,128]{1,0:T(8,128)S(1)}, u32[]{:S(2)}, u32[]{:S(2)}) %collective-permute-start.6) | collective-permute-done | bytes 8224 | tf_op jit(solution)/shard_map/ppermute | solution.py:21
  104.7 0.0 copy-start.4
  104.7 0.0 collective-permute-done.5.pn_ref
  104.7 0.0 copy-start.5
  104.7 0.0 collective-permute-done.3.nxt_ref
  104.7 0.0 copy-start
  104.7 0.0 collective-permute-done.4.prv_ref
  104.7 0.6 copy-done.4
  105.3 0.0 copy-done.5
  105.3 0.4 copy-done
  105.7 0.0 copy-start.1
  105.7 1.0 copy-done.1
  106.7 7.3 %shard_map.102 = bf16[20,400,128]{2,1,0:T(8,128)(2,1)} custom-call(f32[32]{0:T(128)} %pad_maximum_fusion.1.sc_ref, f32[2,10,400,128]{3,2,1,0:T(8,128)} %shard_map.100.part_ref, bf16[20,208,128]{2,1,0:T(8,128)(2,1)} %copy-done, bf16[20,208,128]{2,1,0:T(8,128)(2,1)} %copy-done.1, bf16[20,200,128]{2,1,0:T(8,128)(2,1)} %constant.141.clone.rec_lo.rec_hi.rec_ref, ...), custom_call_target="tpu_custom_call" | custom-call | tf_op jit(solution)/shard_map/pallas_call | solution.py:345
  (6 shorter events, 0.0 us)
Async XLA Ops:
  1.5 1.8 %copy-start.2 = (bf16[39,8000]{1,0:T(8,128)(2,1)S(1)}, bf16[39,8000]{1,0:T(8,128)(2,1)}, u32[]{:S(2)}) copy-start(bf16[39,8000]{1,0:T(8,128)(2,1)} %constant.139.clone) | copy-start | bytes 1872004
  3.3 75.9 %copy-start.6 = (f32[20]{0:T(128)S(1)}, f32[20]{0:T(128)}, u32[]{:S(2)}) copy-start(f32[20]{0:T(128)} %constant.140.clone) | copy-start | bytes 244
  3.8 78.0 %collective-permute-start.1 = (f32[13,128]{1,0:T(8,128)S(1)}, f32[13,128]{1,0:T(8,128)S(1)}, u32[]{:S(2)}, u32[]{:S(2)}) collective-permute-start(f32[13,128]{1,0:T(8,128)S(1)} %slice_add_fusion), channel_id=1, source_target_pairs={{0,2},{1,3},{2,0},{3,1},{4,6},{5,7},{6,4},{7,5},{8,10},{9,11},{10,... | collective-permute-start | bytes 19976 | tf_op jit(solution)/shard_map/ppermute | solution.py:21
  8.0 73.8 %collective-permute-start = (f32[13,128]{1,0:T(8,128)S(1)}, f32[13,128]{1,0:T(8,128)S(1)}, u32[]{:S(2)}, u32[]{:S(2)}) collective-permute-start(f32[13,128]{1,0:T(8,128)S(1)} %slice_add_fusion), channel_id=1, source_target_pairs={{0,1},{1,2},{2,3},{3,0},{4,5},{5,6},{6,7},{7,4},{8,9},{9,10},{10,1... | collective-permute-start | bytes 19976 | tf_op jit(solution)/shard_map/ppermute | solution.py:21
  9.5 72.3 %collective-permute-start.2 = (f32[13,128]{1,0:T(8,128)S(1)}, f32[13,128]{1,0:T(8,128)S(1)}, u32[]{:S(2)}, u32[]{:S(2)}) collective-permute-start(f32[13,128]{1,0:T(8,128)S(1)} %slice_add_fusion), channel_id=1, source_target_pairs={{0,3},{1,0},{2,1},{3,2},{4,7},{5,4},{6,5},{7,6},{8,11},{9,8},{10,9... | collective-permute-start | bytes 19976 | tf_op jit(solution)/shard_map/ppermute | solution.py:21
  77.4 27.3 %collective-permute-start.3 = (bf16[20,208,128]{2,1,0:T(8,128)(2,1)}, bf16[20,208,128]{2,1,0:T(8,128)(2,1)S(1)}, u32[]{:S(2)}, u32[]{:S(2)}) collective-permute-start(bf16[20,208,128]{2,1,0:T(8,128)(2,1)} %get-tuple-element.7), channel_id=1, source_target_pairs={{0,28},{4,0},{8,4},{12,8},{16,12},{20,16},{24,20},{28,24},{1,29},{... | collective-permute-start | bytes 3194888 | tf_op jit(solution)/shard_map/ppermute | solution.py:21
  78.5 26.2 %collective-permute-start.4 = (bf16[20,208,128]{2,1,0:T(8,128)(2,1)}, bf16[20,208,128]{2,1,0:T(8,128)(2,1)S(1)}, u32[]{:S(2)}, u32[]{:S(2)}) collective-permute-start(bf16[20,208,128]{2,1,0:T(8,128)(2,1)} %get-tuple-element.8), channel_id=1, source_target_pairs={{0,4},{4,8},{8,12},{12,16},{16,20},{20,24},{24,28},{28,0},{1,5},{5... | collective-permute-start | bytes 3194888 | tf_op jit(solution)/shard_map/ppermute | solution.py:21
  82.0 4.2 %copy-start.3 = (f32[16,128]{1,0:T(8,128)}, f32[16,128]{1,0:T(8,128)S(1)}, u32[]{:S(2)}) copy-start(f32[16,128]{1,0:T(8,128)S(1)} %maximum_maximum_fusion.pk_ref) | copy-start | bytes 24580
  82.0 22.7 %collective-permute-start.6 = (f32[16,128]{1,0:T(8,128)S(1)}, f32[16,128]{1,0:T(8,128)S(1)}, u32[]{:S(2)}, u32[]{:S(2)}) collective-permute-start(f32[16,128]{1,0:T(8,128)S(1)} %maximum_maximum_fusion.pk_ref), channel_id=1, source_target_pairs={{0,4},{4,8},{8,12},{12,16},{16,20},{20,24},{24,28},{28,0},{1,5},{5... | collective-permute-start | bytes 24584 | tf_op jit(solution)/shard_map/ppermute | solution.py:21
  82.6 22.1 %collective-permute-start.5 = (f32[16,128]{1,0:T(8,128)S(1)}, f32[16,128]{1,0:T(8,128)S(1)}, u32[]{:S(2)}, u32[]{:S(2)}) collective-permute-start(f32[16,128]{1,0:T(8,128)S(1)} %maximum_maximum_fusion.pk_ref), channel_id=1, source_target_pairs={{0,28},{4,0},{8,4},{12,8},{16,12},{20,16},{24,20},{28,24},{1,29},{... | collective-permute-start | bytes 24584 | tf_op jit(solution)/shard_map/ppermute | solution.py:21
  104.7 0.6 copy-start.4
  104.7 0.6 copy-start.5
  104.7 1.0 copy-start
  105.7 1.0 copy-start.1
